TPU v7x, 256 devices: a whole 4x4x8 slice. The times are simulated.
256 devices in a mesh: wide: 32 (over z, x), narrow: 8 (over y, core).
Axes of the slice: x: 4, y: 4, z: 8, core: 2. Of those that a mesh axis runs over, the one named last changes fastest.
Arguments:
- hidden_in: bfloat16 [64, 8192], P(None, 'wide'), may hold values from -6 to 6
- attn_gain: bfloat16 [8192], P('wide'), may hold values from 0.099609375 to 1.8984375
- qkv_weight: bfloat16 [8192, 8, 10, 128], P('wide', 'narrow'), may hold values from -2 to 2
- qkv_bias: bfloat16 [8, 10, 128], P('narrow'), may hold values from -3 to 3
- cache_keys: bfloat16 [64, 8, 4096, 128], P('wide', 'narrow'), may hold values from -256 to 256
- cache_values: bfloat16 [64, 8, 4096, 128], P('wide', 'narrow'), may hold values from -10 to 10
- positions: int32 [64, 3, 4096], P('wide'), may hold values from 0 to 4095
- lengths: int32 [64], P('wide'), may hold values from 512 to 4095, as said below
- out_weight: bfloat16 [8192, 8192], P('narrow', 'wide'), may hold values from -0.0625 to 0.0625
- mlp_gain: bfloat16 [8192], P('wide'), may hold values from 0.099609375 to 1.8984375
- gate_up_weight: bfloat16 [8192, 2, 29568], P('wide', None, 'narrow'), may hold values from -0.0625 to 0.0625
- down_weight: bfloat16 [29568, 8192], P('narrow', 'wide'), may hold values from -0.03125 to 0.03125
Outputs:
- layer_out: bfloat16 [64, 8192], P(None, 'wide')
Inputs may be any that keep to these rules, and one draw needn't show every extreme that they name: Slots 0 to lengths[b] - 1 of request b are filled, the new token takes slot lengths[b], and some request has 4095.
All inputs are finite; a program needn't handle non-finite values.
Results may differ from a plain program's by a relative error of at most 0.01115.
The roundings to bfloat16 on the way count: a program that leaves them out, or rounds other values in their place, can miss the bound.
Values may be sent and summed in bfloat16 or wider, within the bound.
No kernel may reach another device: no remote copies, remote signals or barrier semaphores. Data moves between devices by JAX's collectives and lax.ppermute only.
A program may use at most 64 MiB of HBM per device.

v0:
```python
import math
import jax
import jax.numpy as jnp
from jax import lax
from jax.sharding import PartitionSpec as P

D = 8192
DH = 128
CACHE = 4096
norm_eps = 1e-06
rope_base = 1000000.0


def mrope_tables(position):
    half_width = DH // 2
    pair_index = jnp.arange(half_width)
    inv_freq = jnp.exp(pair_index.astype(jnp.float32) * (-2.0 * math.log(rope_base) / DH))
    component = (pair_index >= DH // 8).astype(jnp.int32) + (
        pair_index >= DH // 8 + 3 * DH // 16
    ).astype(jnp.int32)
    pos_float = position.astype(jnp.float32)
    chosen = jnp.where(
        component == 0,
        pos_float[..., 0, :, None],
        jnp.where(component == 1, pos_float[..., 1, :, None], pos_float[..., 2, :, None]),
    )
    angles = chosen * inv_freq
    return (jnp.cos(angles), jnp.sin(angles))


def rotate(values, cosine, sine_table):
    half_width = values.shape[-1] // 2
    leading = values[..., :half_width]
    trailing = values[..., half_width:]
    return jnp.concatenate(
        [leading * cosine - trailing * sine_table, trailing * cosine + leading * sine_table],
        axis=-1,
    )


def local(
    hidden_in,
    attn_gain,
    qkv_weight,
    qkv_bias,
    cache_keys,
    cache_values,
    positions,
    lengths,
    out_weight,
    mlp_gain,
    gate_up_weight,
    down_weight,
):
    score_scale = 1.0 / math.sqrt(DH)
    owned = lengths.shape[0]
    local_rows = hidden_in.shape[1]
    kv_local = qkv_weight.shape[1]
    slot_count = qkv_weight.shape[2]
    group_size = slot_count - 2
    width = kv_local * slot_count * DH
    inputs = hidden_in.astype(jnp.float32)
    local_squares = jnp.sum(inputs * inputs, axis=1)
    scaled = (inputs * attn_gain.astype(jnp.float32)).astype(jnp.bfloat16)
    weight_flat = qkv_weight.reshape(local_rows, width)
    inv_rms = 1.0 / jnp.sqrt(lax.psum(local_squares, "wide") / D + norm_eps)
    row_block = scaled
    factor = inv_rms
    projected = lax.psum_scatter(
        factor[:, None] * jnp.dot(row_block, weight_flat, preferred_element_type=jnp.float32),
        "wide",
        scatter_dimension=0,
        tiled=True,
    )
    projected = projected + qkv_bias.reshape(width).astype(jnp.float32)
    projected = projected.reshape(owned, kv_local, slot_count, DH)
    cosine, sine_table = mrope_tables(positions)
    keys_rot = rotate(cache_keys.astype(jnp.float32), cosine[:, None], sine_table[:, None]).astype(
        jnp.bfloat16
    )
    new_position = jnp.take_along_axis(positions, lengths[:, None, None], axis=2)
    cos_new, sin_new = mrope_tables(new_position)
    query = rotate(projected[:, :, :group_size], cos_new[:, None], sin_new[:, None]).astype(
        jnp.bfloat16
    )
    key_new = rotate(projected[:, :, group_size], cos_new, sin_new).astype(jnp.bfloat16)
    value_new = projected[:, :, group_size + 1].astype(jnp.bfloat16)
    scores = (
        jnp.einsum("rgjd,rgsd->rgjs", query, keys_rot, preferred_element_type=jnp.float32)
        * score_scale
    )
    own_score = (
        jnp.sum(query.astype(jnp.float32) * key_new.astype(jnp.float32)[:, :, None, :], axis=3)
        * score_scale
    )
    valid_slot = jnp.arange(CACHE)[None, None, None, :] < lengths[:, None, None, None]
    row_max = jnp.maximum(jnp.max(jnp.where(valid_slot, scores, -jnp.inf), axis=3), own_score)
    probabilities = jnp.where(valid_slot, jnp.exp(scores - row_max[..., None]), 0.0)
    own_prob = jnp.exp(own_score - row_max)
    totals = jnp.sum(probabilities, axis=3) + own_prob
    probs_rounded = probabilities.astype(jnp.bfloat16)
    own_rounded = own_prob.astype(jnp.bfloat16).astype(jnp.float32)
    weighted = jnp.einsum(
        "rgjs,rgsd->rgjd", probs_rounded, cache_values, preferred_element_type=jnp.float32
    )
    weighted = weighted + own_rounded[..., None] * value_new.astype(jnp.float32)[:, :, None, :]
    attended = (
        (weighted / totals[..., None])
        .astype(jnp.bfloat16)
        .reshape(owned, kv_local * group_size * DH)
    )
    head_partial = jnp.dot(
        lax.all_gather(attended, "wide", axis=0, tiled=True),
        out_weight,
        preferred_element_type=jnp.float32,
    )
    attn_out = lax.psum(head_partial, "narrow")
    residual = (inputs + attn_out).astype(jnp.bfloat16)
    resid_float = residual.astype(jnp.float32)
    resid_squares = jnp.sum(resid_float * resid_float, axis=1)
    scaled2 = (resid_float * mlp_gain.astype(jnp.float32)).astype(jnp.bfloat16)
    hidden_local = gate_up_weight.shape[2]
    gate_up_flat = gate_up_weight.reshape(local_rows, 2 * hidden_local)
    inv_rms2 = 1.0 / jnp.sqrt(lax.psum(resid_squares, "wide") / D + norm_eps)
    row_block = scaled2
    factor = inv_rms2
    gate_up = lax.psum_scatter(
        factor[:, None] * jnp.dot(row_block, gate_up_flat, preferred_element_type=jnp.float32),
        "wide",
        scatter_dimension=0,
        tiled=True,
    )
    hidden = (jax.nn.silu(gate_up[:, :hidden_local]) * gate_up[:, hidden_local:]).astype(
        jnp.bfloat16
    )
    down_partial = jnp.dot(
        lax.all_gather(hidden, "wide", axis=0, tiled=True),
        down_weight,
        preferred_element_type=jnp.float32,
    )
    mlp_out = lax.psum(down_partial, "narrow")
    return (resid_float + mlp_out).astype(jnp.bfloat16)


def solution(mesh):
    in_specs = (
        P(None, "wide"),
        P("wide"),
        P("wide", "narrow", None, None),
        P("narrow", None, None),
        P("wide", "narrow", None, None),
        P("wide", "narrow", None, None),
        P("wide", None, None),
        P("wide"),
        P("narrow", "wide"),
        P("wide"),
        P("wide", None, "narrow"),
        P("narrow", "wide"),
    )
    out_specs = P(None, "wide")
    return jax.shard_map(local, mesh=mesh, in_specs=in_specs, out_specs=out_specs, check_vma=False)
```

profile of v0, /device:TPU:2, one launch (start us, length us, event | category | flops | bytes accessed | tf_op | source)
XLA Modules:
  0.0 691.7 jit_solution(1203411043637431055)
XLA Ops:
  6.5 1.5 copy.20
  8.0 0.9 fusion.24
  8.9 73.7 %psum.28 = f32[64]{0:T(128)S(1)} all-reduce(f32[64]{0:T(128)S(1)} %fusion.24), channel_id=1, replica_groups=mesh['wide'=32,'narrow'=8] {'wide'}, use_global_device_ids=true, to_apply=%region_1.0 | all-reduce | flops 64 | bytes 512 | tf_op jit(solution)/shard_map/psum | solution.py:66
  83.3 1.8 convolution_multiply_fusion.2
  85.2 0.9 convert_element_type.179
  86.1 3.4 copy.22
  89.7 3.8 bitcast_convert_fusion
  93.8 1.4 gather_fusion
  95.6 19.8 %fusion.7 = (bf16[2,4096,64]{2,1,0:T(8,128)(2,1)}, bf16[2,4096,64]{2,1,0:T(8,128)(2,1)}) fusion(f32[2,1,4096,128]{3,2,0,1:T(8,128)} %bitcast_convert_fusion, f32[64]{0:T(128)S(1)} %multiply_exponential_fusion, f32[2,4096]{1,0:T(2,128)S(1)} %get-tuple-element.17, f32[2,4096]{1,0:T(2,128)S(1)} %get-tuple-element.18, f32[2,4096]{1,0:T(2,128)S(1)} %get-tuple-element.16, ...), kind=kLoop, calls=%fused_computation.15 | loop fusion | flops 5767168 | bytes 6390144 | tf_op jit(solution)/shard_map/concatenate | solution.py:35
  116.8 112.9 %all-reduce.11.cloned.1.call-done = f32[64,1280]{1,0:T(8,128)} async-done(((f32[64,1280]{1,0:T(8,128)}), f32[64,1280]{1,0:T(8,128)}) %all-reduce.11.cloned.1.call-update) | async-done | bytes 327696
  229.7 0.8 dynamic-slice_add_fusion
  231.0 3.6 select_reduce_fusion
  235.3 41.5 %all-gather = bf16[32,2,1024]{2,1,0:T(2,128)(2,1)S(1)} all-gather(bf16[1,2,1024]{2,1,0:T(2,128)(2,1)S(1)} %reshape.655), channel_id=1, replica_groups=mesh['wide'=32,'narrow'=8] {'wide'}, dimensions={0}, use_global_device_ids=true | all-gather | bytes 135168 | tf_op jit(solution)/shard_map/all_gather | solution.py:113
  276.9 0.8 fusion.52
  277.8 63.5 %all-reduce.7.cloned.1.call-done = f32[64,256]{1,0:T(8,128)} async-done(((f32[64,256]{1,0:T(8,128)}), f32[64,256]{1,0:T(8,128)}) %all-reduce.7.cloned.1.call-update) | async-done | bytes 65552 | tf_op jit(solution)/shard_map/psum | solution.py:117
  341.3 0.9 fusion.27
  342.3 71.1 %psum.30 = f32[64]{0:T(128)S(1)} all-reduce(f32[64]{0:T(128)S(1)} %get-tuple-element.8), channel_id=1, replica_groups=mesh['wide'=32,'narrow'=8] {'wide'}, use_global_device_ids=true, to_apply=%region_8.9 | all-reduce | flops 64 | bytes 512 | tf_op jit(solution)/shard_map/psum | solution.py:124
  413.4 4.6 convolution_multiply_fusion
  418.1 149.5 %all-reduce.13.cloned.1.call-done = f32[64,7392]{1,0:T(8,128)} async-done(((f32[64,7392]{1,0:T(8,128)}), f32[64,7392]{1,0:T(8,128)}) %all-reduce.13.cloned.1.call-update) | async-done | bytes 1892368
  567.6 1.1 fusion.36
  568.7 48.7 %all-gather.1 = bf16[32,2,3696]{2,1,0:T(2,128)(2,1)S(1)} all-gather(bf16[1,2,3696]{2,1,0:T(2,128)(2,1)S(1)} %fusion.36), channel_id=1, replica_groups=mesh['wide'=32,'narrow'=8] {'wide'}, dimensions={0}, use_global_device_ids=true | all-gather | bytes 487872 | tf_op jit(solution)/shard_map/all_gather | solution.py:137
  617.7 2.6 fusion.53
  620.3 63.4 %all-reduce.9.cloned.1.call-done = f32[64,256]{1,0:T(8,128)} async-done(((f32[64,256]{1,0:T(8,128)}), f32[64,256]{1,0:T(8,128)}) %all-reduce.9.cloned.1.call-update) | async-done | bytes 65552 | tf_op jit(solution)/shard_map/psum | solution.py:141
  683.7 1.5 fusion.29
  (57 shorter events, 4.0 us)
Async XLA Ops:
  6.5 228.3 %copy-start = (bf16[2,1,4096,128]{3,2,1,0:T(8,128)(2,1)S(1)}, bf16[2,1,4096,128]{3,2,1,0:T(8,128)(2,1)}, u32[]{:S(2)}) copy-start(bf16[2,1,4096,128]{3,2,1,0:T(8,128)(2,1)} %param.17) | copy-start | bytes 6291460
  6.5 83.0 %copy-start.4 = (s32[2]{0:T(128)S(1)}, s32[2]{0:T(128)}, u32[]{:S(2)}) copy-start(s32[2]{0:T(128)} %param.19) | copy-start | bytes 28
  6.5 223.2 %all-reduce.11.cloned.1.call-start = ((), (), s32[]{:S(2)}) async-start(), calls=%async_computation.2 | async-start | bytes 655360
  85.1 256.2 %all-reduce.7.cloned.1.call-start = ((), (), s32[]{:S(2)}) async-start(), calls=%async_computation | async-start | bytes 131072 | tf_op jit(solution)/shard_map/psum | solution.py:117
  95.6 20.0 %copy-start.6 = (u32[256]{0:T(256)S(1)}, u32[256]{0:T(256)}, u32[]{:S(2)}) copy-start(u32[256]{0:T(256)} %constant.61) | copy-start | bytes 3076
  95.6 21.2 %copy-start.3 = (bf16[1,10,128]{2,1,0:T(8,128)(2,1)S(1)}, bf16[1,10,128]{2,1,0:T(8,128)(2,1)}, u32[]{:S(2)}) copy-start(bf16[1,10,128]{2,1,0:T(8,128)(2,1)} %param.15) | copy-start | bytes 7684
  231.0 45.9 %copy-start.1 = (bf16[1024,256]{1,0:T(8,128)(2,1)S(1)}, bf16[1024,256]{1,0:T(8,128)(2,1)}, u32[]{:S(2)}) copy-start(bf16[1024,256]{1,0:T(8,128)(2,1)} %param.20) | copy-start | bytes 1572868
  231.0 46.8 %copy-start.5 = (bf16[256]{0:T(256)(128)(2,1)S(1)}, bf16[256]{0:T(256)(128)(2,1)}, u32[]{:S(2)}) copy-start(bf16[256]{0:T(256)(128)(2,1)} %param.21) | copy-start | bytes 1540
  231.0 110.4 %copy-start.2 = (bf16[64,256]{1,0:T(8,128)(2,1)S(1)}, bf16[64,256]{1,0:T(8,128)(2,1)}, u32[]{:S(2)}) copy-start(bf16[64,256]{1,0:T(8,128)(2,1)} %param.12) | copy-start | bytes 98308
  277.7 289.9 %all-reduce.13.cloned.1.call-start = ((), (), s32[]{:S(2)}) async-start(), calls=%async_computation.3 | async-start | bytes 3801088
  418.0 265.6 %all-reduce.9.cloned.1.call-start = ((), (), s32[]{:S(2)}) async-start(), calls=%async_computation.1 | async-start | bytes 131072 | tf_op jit(solution)/shard_map/psum | solution.py:141
Sparse Core Ops, SparseCore 0:
  85.3 144.4 all-reduce.10
  277.9 63.4 all-reduce.6
  418.2 149.3 all-reduce.12
  620.4 63.1 all-reduce.8
where the time goes:
time: 692 us
  waiting for transfers between devices  389 us (56%)
  blocking collectives  235 us (34%)
  other arithmetic  31.6 us (5%)
  between operations  14 us (2%)
  matrix products  13.9 us (2%)
  local copies, waits for them, and re-layouts  7.72 us (1%)
    unnamed x6, waiting for transfers between devices  262 us
    psum x1, blocking collectives, local(): inv_rms = 1.0 / jnp.sqrt(lax.psum(local_squares, 'wide') / D + norm_eps)  73.7 us
    psum x1, blocking collectives, local(): inv_rms2 = 1.0 / jnp.sqrt(lax.psum(resid_squares, 'wide') / D + norm_eps)  71.1 us
    psum x1, waiting for transfers between devices, local(): attn_out = lax.psum(head_partial, 'narrow')  63.5 us
    psum x1, waiting for transfers between devices, local(): mlp_out = lax.psum(down_partial, 'narrow')  63.4 us
    all_gather x1, blocking collectives, local(): lax.all_gather(hidden, 'wide', axis=0, tiled=True)  48.7 us
    all_gather x1, blocking collectives, local(): lax.all_gather(attended, 'wide', axis=0, tiled=True)  41.5 us
    concatenate x2, other arithmetic, rotate(): jnp.concatenate([leading * cosine - trailing * sine_table, trailing * cos...  19.8 us
  transfers between devices with their start and end apart: 4, of which 4 were waited for; matrix products, arithmetic and copies ran while one was open for 4% of the time, Pallas kernels for 0%

commit v1 on v0

--- a/solution.py
+++ b/solution.py
@@ -138,7 +138,9 @@
         down_weight,
         preferred_element_type=jnp.float32,
     )
-    mlp_out = lax.psum(down_partial, "narrow")
+    mlp_out = down_partial
+    for hop in (1, 2, 4):
+        mlp_out = mlp_out + lax.ppermute(mlp_out, "narrow", [(dev, dev ^ hop) for dev in range(8)])
     return (resid_float + mlp_out).astype(jnp.bfloat16)
 
 

time: 692 us -> 640 us (0.925)
  waiting for transfers between devices: 389 us -> 333 us
    psum x1 -> x0, waiting for transfers between devices: 63.4 us -> none  [local(): mlp_out = lax.psum(down_partial, 'narrow')]
    unnamed x6 -> x5, waiting for transfers between devices: 262 us -> 262 us
  transfers between devices with their start and end apart: 4 -> 6, of which waited for: 4 -> 6; matrix products, arithmetic and copies ran while one was open for 4% -> 5% of each run, Pallas kernels for 0% -> 0%
where the time goes in v1:
time: 640 us; the launch traced here: 638 us
  waiting for transfers between devices  333 us (52%)
  blocking collectives  235 us (37%)
  other arithmetic  30.8 us (5%)
  between operations  14 us (2%)
  matrix products  13.3 us (2%)
  local copies, waits for them, and re-layouts  7.72 us (1%)
    unnamed x5, waiting for transfers between devices  262 us
    psum x1, blocking collectives, local(): inv_rms = 1.0 / jnp.sqrt(lax.psum(local_squares, 'wide') / D + norm_eps)  73.7 us
    psum x1, blocking collectives, local(): inv_rms2 = 1.0 / jnp.sqrt(lax.psum(resid_squares, 'wide') / D + norm_eps)  71.1 us
    psum x1, waiting for transfers between devices, local(): attn_out = lax.psum(head_partial, 'narrow')  63.5 us
    all_gather x1, blocking collectives, local(): lax.all_gather(hidden, 'wide', axis=0, tiled=True)  48.7 us
    all_gather x1, blocking collectives, local(): lax.all_gather(attended, 'wide', axis=0, tiled=True)  41.5 us
    concatenate x2, other arithmetic, rotate(): jnp.concatenate([leading * cosine - trailing * sine_table, trailing * cos...  19.8 us
  transfers between devices with their start and end apart: 6, of which 6 were waited for; matrix products, arithmetic and copies ran while one was open for 5% of the time, Pallas kernels for 0%

profile of v1, /device:TPU:2, one launch (start us, length us, event | category | flops | bytes accessed | tf_op | source)
XLA Modules:
  0.0 638.4 jit_solution(13457229106401969257)
XLA Ops:
  6.5 1.5 copy.20
  8.9 73.7 %psum.21 = f32[64]{0:T(128)S(1)} all-reduce(f32[64]{0:T(128)S(1)} %fusion.24), channel_id=1, replica_groups=mesh['wide'=32,'narrow'=8] {'wide'}, use_global_device_ids=true, to_apply=%region_1.0 | all-reduce | flops 64 | bytes 512 | tf_op jit(solution)/shard_map/psum | solution.py:66
  83.3 1.8 convolution_multiply_fusion.2
  85.2 0.9 convert_element_type.179
  86.1 3.4 copy.22
  89.7 3.8 bitcast_convert_fusion
  93.8 1.4 gather_fusion
  95.6 19.8 %fusion.7 = (bf16[2,4096,64]{2,1,0:T(8,128)(2,1)}, bf16[2,4096,64]{2,1,0:T(8,128)(2,1)}) fusion(f32[2,1,4096,128]{3,2,0,1:T(8,128)} %bitcast_convert_fusion, f32[64]{0:T(128)S(1)} %multiply_exponential_fusion, f32[2,4096]{1,0:T(2,128)S(1)} %get-tuple-element.17, f32[2,4096]{1,0:T(2,128)S(1)} %get-tuple-element.18, f32[2,4096]{1,0:T(2,128)S(1)} %get-tuple-element.16, ...), kind=kLoop, calls=%fused_computation.15 | loop fusion | flops 5767168 | bytes 6390144 | tf_op jit(solution)/shard_map/concatenate | solution.py:35
  116.8 112.9 %all-reduce.8.cloned.1.call-done = f32[64,1280]{1,0:T(8,128)} async-done(((f32[64,1280]{1,0:T(8,128)}), f32[64,1280]{1,0:T(8,128)}) %all-reduce.8.cloned.1.call-update) | async-done | bytes 327696
  231.0 3.6 select_reduce_fusion
  235.3 41.5 %all-gather = bf16[32,2,1024]{2,1,0:T(2,128)(2,1)S(1)} all-gather(bf16[1,2,1024]{2,1,0:T(2,128)(2,1)S(1)} %reshape.655), channel_id=1, replica_groups=mesh['wide'=32,'narrow'=8] {'wide'}, dimensions={0}, use_global_device_ids=true | all-gather | bytes 135168 | tf_op jit(solution)/shard_map/all_gather | solution.py:113
  277.8 63.5 %all-reduce.6.cloned.1.call-done = f32[64,256]{1,0:T(8,128)} async-done(((f32[64,256]{1,0:T(8,128)}), f32[64,256]{1,0:T(8,128)}) %all-reduce.6.cloned.1.call-update) | async-done | bytes 65552 | tf_op jit(solution)/shard_map/psum | solution.py:117
  341.3 0.9 fusion.27
  342.3 71.1 %psum.23 = f32[64]{0:T(128)S(1)} all-reduce(f32[64]{0:T(128)S(1)} %get-tuple-element.8), channel_id=1, replica_groups=mesh['wide'=32,'narrow'=8] {'wide'}, use_global_device_ids=true, to_apply=%region_8.9 | all-reduce | flops 64 | bytes 512 | tf_op jit(solution)/shard_map/psum | solution.py:124
  413.4 4.6 convolution_multiply_fusion
  418.0 149.5 %all-reduce.10.cloned.1.call-done = f32[64,7392]{1,0:T(8,128)} async-done(((f32[64,7392]{1,0:T(8,128)}), f32[64,7392]{1,0:T(8,128)}) %all-reduce.10.cloned.1.call-update) | async-done | bytes 1892368
  567.6 1.1 fusion.36
  568.7 48.7 %all-gather.1 = bf16[32,2,3696]{2,1,0:T(2,128)(2,1)S(1)} all-gather(bf16[1,2,3696]{2,1,0:T(2,128)(2,1)S(1)} %fusion.36), channel_id=1, replica_groups=mesh['wide'=32,'narrow'=8] {'wide'}, dimensions={0}, use_global_device_ids=true | all-gather | bytes 487872 | tf_op jit(solution)/shard_map/all_gather | solution.py:137
  617.7 2.0 fusion.53
  619.8 1.2 collective-permute-done
  621.0 1.6 collective-permute-start.1
  622.6 2.8 collective-permute-done.1
  625.4 3.1 collective-permute-start.2
  628.5 2.8 collective-permute-done.2
  (62 shorter events, 7.1 us)
Async XLA Ops:
  6.5 228.3 %copy-start = (bf16[2,1,4096,128]{3,2,1,0:T(8,128)(2,1)S(1)}, bf16[2,1,4096,128]{3,2,1,0:T(8,128)(2,1)}, u32[]{:S(2)}) copy-start(bf16[2,1,4096,128]{3,2,1,0:T(8,128)(2,1)} %param.17) | copy-start | bytes 6291460
  6.5 83.0 %copy-start.4 = (s32[2]{0:T(128)S(1)}, s32[2]{0:T(128)}, u32[]{:S(2)}) copy-start(s32[2]{0:T(128)} %param.19) | copy-start | bytes 28
  6.5 223.2 %all-reduce.8.cloned.1.call-start = ((), (), s32[]{:S(2)}) async-start(), calls=%async_computation.1 | async-start | bytes 655360
  85.1 256.2 %all-reduce.6.cloned.1.call-start = ((), (), s32[]{:S(2)}) async-start(), calls=%async_computation | async-start | bytes 131072 | tf_op jit(solution)/shard_map/psum | solution.py:117
  95.6 20.0 %copy-start.6 = (u32[256]{0:T(256)S(1)}, u32[256]{0:T(256)}, u32[]{:S(2)}) copy-start(u32[256]{0:T(256)} %constant.61) | copy-start | bytes 3076
  95.6 21.2 %copy-start.3 = (bf16[1,10,128]{2,1,0:T(8,128)(2,1)S(1)}, bf16[1,10,128]{2,1,0:T(8,128)(2,1)}, u32[]{:S(2)}) copy-start(bf16[1,10,128]{2,1,0:T(8,128)(2,1)} %param.15) | copy-start | bytes 7684
  231.0 45.9 %copy-start.1 = (bf16[1024,256]{1,0:T(8,128)(2,1)S(1)}, bf16[1024,256]{1,0:T(8,128)(2,1)}, u32[]{:S(2)}) copy-start(bf16[1024,256]{1,0:T(8,128)(2,1)} %param.20) | copy-start | bytes 1572868
  231.0 46.8 %copy-start.5 = (bf16[256]{0:T(256)(128)(2,1)S(1)}, bf16[256]{0:T(256)(128)(2,1)}, u32[]{:S(2)}) copy-start(bf16[256]{0:T(256)(128)(2,1)} %param.21) | copy-start | bytes 1540
  231.0 110.4 %copy-start.2 = (bf16[64,256]{1,0:T(8,128)(2,1)S(1)}, bf16[64,256]{1,0:T(8,128)(2,1)}, u32[]{:S(2)}) copy-start(bf16[64,256]{1,0:T(8,128)(2,1)} %param.12) | copy-start | bytes 98308
  277.7 289.9 %all-reduce.10.cloned.1.call-start = ((), (), s32[]{:S(2)}) async-start(), calls=%async_computation.2 | async-start | bytes 3801088
  619.7 1.3 collective-permute-start
  621.0 4.4 collective-permute-start.1
  625.4 5.9 collective-permute-start.2
Sparse Core Ops, SparseCore 0:
  85.3 144.4 all-reduce.7
  277.9 63.4 all-reduce.5
  418.2 149.3 all-reduce.9
